TPU v7x, 512 devices: a whole 4x4x16 slice. The times are simulated.
512 devices in a mesh: dp: 32 (over y, x, core), tensor: 16 (over z).
Axes of the slice: x: 4, y: 4, z: 16, core: 2. Of those that a mesh axis runs over, the one named last changes fastest.
Arguments:
- activations: bfloat16 [32768, 4096], P('dp', 'tensor'), may hold values from -40 to 40
- labels: int32 [32768], P('dp'), may hold values from 0 to 7, as said below
Outputs:
- covariance: float32 [4096, 4096], P('tensor', 'dp')
- cross_covariance: float32 [8, 4096], P(None, 'tensor')
Inputs may be any that keep to these rules, and one draw needn't show every extreme that they name: Every one of the 8 classes labels at least one token.
All inputs are finite; a program needn't handle non-finite values.
Results may differ from a plain program's by a relative error of at most 0.0003.
Values may be sent and summed in bfloat16 or wider, within the bound.
No kernel may reach another device: no remote copies, remote signals or barrier semaphores. Data moves between devices by JAX's collectives and lax.ppermute only.
A program may use at most 64 MiB of HBM per device.

v0:
```python
import jax
import jax.numpy as jnp
from jax import lax
from jax.sharding import PartitionSpec as P

D = 4096
CLASSES = 8


def body(activations, labels):
    tok_rows, slice_width = activations.shape
    token_total = tok_rows * lax.axis_size("dp")
    col_width = D // lax.axis_size("dp")
    classes = jnp.arange(CLASSES, dtype=jnp.int32)
    matches = labels[None, :] == classes[:, None]
    onehot = matches.astype(jnp.bfloat16)
    local_counts = jnp.sum(matches.astype(jnp.float32), axis=1)
    gathered = lax.all_gather(activations, "tensor", axis=1, tiled=True)
    gram_cols = lax.psum_scatter(
        lax.dot_general(
            gathered, activations, (((0,), (0,)), ((), ())), preferred_element_type=jnp.float32
        ),
        "dp",
        scatter_dimension=0,
        tiled=True,
    )
    slice_start = lax.axis_index("tensor") * slice_width
    wide_local = jnp.dot(onehot, gathered, preferred_element_type=jnp.float32)
    class_sums, class_counts = lax.psum((wide_local, local_counts), "dp")
    own_sums = lax.dynamic_slice_in_dim(class_sums, slice_start, slice_width, 1)
    overall_mean = jnp.sum(class_sums, axis=0) / token_total
    mean_rows = lax.dynamic_slice_in_dim(overall_mean, slice_start, slice_width, 0)
    mean_cols = lax.dynamic_slice_in_dim(
        overall_mean, lax.axis_index("dp") * col_width, col_width, 0
    )
    covariance = gram_cols.T / token_total - mean_rows[:, None] * mean_cols[None, :]
    cross_covariance = (own_sums - class_counts[:, None] * mean_rows[None, :]) / token_total
    return (covariance, cross_covariance)


def solution(mesh):
    in_specs = (P("dp", "tensor"), P("dp"))
    out_specs = (P("tensor", "dp"), P(None, "tensor"))
    return jax.shard_map(body, mesh=mesh, in_specs=in_specs, out_specs=out_specs, check_vma=False)
```

profile of v0, /device:TPU:2, one launch (start us, length us, event | category | flops | bytes accessed | tf_op | source)
XLA Modules:
  0.0 394.7 jit_solution(16058188507503878054)
XLA Ops:
  7.2 0.0 copy-start
  7.2 0.0 all-gather.2.cloned.1.call-start
  7.2 0.7 all-gather.2.cloned.1.call-update
  7.9 0.0 all-reduce.2.cloned.1.call-start
  8.0 135.1 %all-gather.2.cloned.1.call-done = bf16[1024,4096]{1,0:T(8,128)(2,1)} async-done(((bf16[1024,256]{1,0:T(8,128)(2,1)}), bf16[1024,4096]{1,0:T(8,128)(2,1)}) %all-gather.2.cloned.1.call-update) | async-done | bytes 8388624 | tf_op jit(solution)/shard_map/all_gather | solution.py:18
  143.1 5.2 %fusion = f32[8,4096]{1,0:T(8,128)} fusion(bf16[1024,4096]{1,0:T(8,128)(2,1)} %all-gather.2.cloned.1.call-done, s32[1024]{0:T(1024)} %param.3), kind=kOutput, calls=%fused_computation.3 | convolution fusion | flops 67117056 | bytes 8523776 | tf_op jit(solution)/shard_map/dot_general | solution.py:28
  148.3 0.0 all-reduce.2.cloned.1.call-update
  148.4 0.0 copy-start.1
  148.4 0.0 reduce-scatter.2.cloned.1.call-start
  148.4 0.0 copy-done
  148.4 7.8 %fusion.2 = f32[4096,256]{1,0:T(8,128)} fusion(bf16[1024,4096]{1,0:T(8,128)(2,1)} %all-gather.2.cloned.1.call-done, bf16[1024,256]{1,0:T(8,128)(2,1)S(1)} %copy-done), kind=kOutput, calls=%fused_computation.7 | convolution fusion | flops 2147483648 | bytes 13107200 | tf_op jit(solution)/shard_map/dot_general | solution.py:20
  156.2 0.0 reduce-scatter.2.cloned.1.call-update
  156.3 0.0 copy-done.1
  156.3 0.1 convert_reduce_fusion
  156.4 57.2 %psum.15 = f32[8]{0:T(128)S(1)} all-reduce(f32[8]{0:T(128)S(1)} %convert_reduce_fusion), channel_id=1, replica_groups=mesh['dp'=32,'tensor'=16] {'dp'}, use_global_device_ids=true, to_apply=%region_4.0 | all-reduce | flops 8 | bytes 64 | tf_op jit(solution)/shard_map/psum | solution.py:29
  213.6 62.8 %all-reduce.2.cloned.1.call-done = f32[8,4096]{1,0:T(8,128)} async-done(((f32[8,4096]{1,0:T(8,128)}), f32[8,4096]{1,0:T(8,128)}) %all-reduce.2.cloned.1.call-update) | async-done | bytes 131088 | tf_op jit(solution)/shard_map/psum | solution.py:29
  276.4 0.9 reduce_sum.18
  277.4 0.1 dynamic_slice.10
  277.5 0.1 dynamic_slice.9
  277.5 1.4 subtract_multiply_fusion
  278.9 107.5 %reduce-scatter.2.cloned.1.call-done = f32[128,256]{1,0:T(8,128)} async-done(((f32[4096,256]{1,0:T(8,128)}), f32[128,256]{1,0:T(8,128)}) %reduce-scatter.2.cloned.1.call-update) | async-done | bytes 131088 | tf_op jit(solution)/shard_map/reduce_scatter | solution.py:19
  386.4 1.0 bitcast_subtract_fusion
  387.4 0.8 copy.5
  (1 shorter events, 0.0 us)
Async XLA Ops:
  7.2 141.3 %copy-start = (bf16[1024,256]{1,0:T(8,128)(2,1)S(1)}, bf16[1024,256]{1,0:T(8,128)(2,1)}, u32[]{:S(2)}) copy-start(bf16[1024,256]{1,0:T(8,128)(2,1)} %param.2) | copy-start | bytes 1572868
  7.2 135.9 %all-gather.2.cloned.1.call-start = ((), (), s32[]{:S(2)}) async-start(), calls=%async_computation.1 | async-start | bytes 8912896 | tf_op jit(solution)/shard_map/all_gather | solution.py:18
  7.9 268.5 %all-reduce.2.cloned.1.call-start = ((), (), s32[]{:S(2)}) async-start(), calls=%async_computation.3 | async-start | bytes 262144 | tf_op jit(solution)/shard_map/psum | solution.py:29
  148.4 7.9 %copy-start.1 = (s32[1024]{0:T(1024)S(1)}, s32[1024]{0:T(1024)}, u32[]{:S(2)}) copy-start(s32[1024]{0:T(1024)} %param.3) | copy-start | bytes 12292
  148.4 238.0 %reduce-scatter.2.cloned.1.call-start = ((), (), s32[]{:S(2)}) async-start(), calls=%async_computation.2 | async-start | bytes 4325376 | tf_op jit(solution)/shard_map/reduce_scatter | solution.py:19
Sparse Core Ops, SparseCore 0:
  10.0 133.0 all-gather.1
  148.5 127.9 all-reduce.1
  281.0 105.3 reduce-scatter.1
where the time goes:
time: 395 us
  waiting for transfers between devices  306 us (77%)
  blocking collectives  57.2 us (14%)
  between operations  13.8 us (3%)
  matrix products  13.1 us (3%)
    all_gather x1, waiting for transfers between devices, body(): gathered = lax.all_gather(activations, 'tensor', axis=1, tiled=True)  135 us
    reduce_scatter x1, waiting for transfers between devices, body(): lax.psum_scatter(lax.dot_general(gathered, activations, (((0,), (0,)), ((...  107 us
    psum x1, waiting for transfers between devices, body(): class_sums, class_counts = lax.psum((wide_local, local_counts), 'dp')  62.8 us
    psum x1, blocking collectives, body(): class_sums, class_counts = lax.psum((wide_local, local_counts), 'dp')  57.2 us
  transfers between devices with their start and end apart: 3, of which 3 were waited for; matrix products, arithmetic and copies ran while one was open for 3% of the time, Pallas kernels for 0%

commit v1 on v0

--- a/solution.py
+++ b/solution.py
@@ -15,7 +15,9 @@
     matches = labels[None, :] == classes[:, None]
     onehot = matches.astype(jnp.bfloat16)
     local_counts = jnp.sum(matches.astype(jnp.float32), axis=1)
-    gathered = lax.all_gather(activations, "tensor", axis=1, tiled=True)
+    gathered = jnp.concatenate(
+        lax.all_to_all(jnp.stack([activations] * lax.axis_size("tensor")), "tensor", 0, 0), axis=1
+    )
     gram_cols = lax.psum_scatter(
         lax.dot_general(
             gathered, activations, (((0,), (0,)), ((), ())), preferred_element_type=jnp.float32

time: 395 us -> 643 us (1.63)
  blocking collectives: 57.2 us -> 439 us
  waiting for transfers between devices: 306 us -> 169 us
    all_to_all x0 -> x1, blocking collectives: none -> 381 us  [body(): lax.all_to_all(jnp.stack([activations] * lax.axis_size('tensor')), 'tenso...]
    all_gather x1 -> x0, waiting for transfers between devices: 135 us -> none  [body(): gathered = lax.all_gather(activations, 'tensor', axis=1, tiled=True)]
  transfers between devices with their start and end apart: 3 -> 2, of which waited for: 3 -> 2; matrix products, arithmetic and copies ran while one was open for 3% -> 2% of each run, Pallas kernels for 0% -> 0%
where the time goes in v1:
time: 643 us
  blocking collectives  439 us (68%)
  waiting for transfers between devices  169 us (26%)
  between operations  14.1 us (2%)
  matrix products  10.6 us (2%)
  local copies, waits for them, and re-layouts  6.48 us (1%)
    all_to_all x1, blocking collectives, body(): lax.all_to_all(jnp.stack([activations] * lax.axis_size('tensor')), 'tenso...  381 us
    reduce_scatter x1, waiting for transfers between devices, body(): lax.psum_scatter(lax.dot_general(gathered, activations, (((0,), (0,)), ((...  107 us
    psum x1, waiting for transfers between devices, body(): class_sums, class_counts = lax.psum((wide_local, local_counts), 'dp')  61.7 us
    psum x1, blocking collectives, body(): class_sums, class_counts = lax.psum((wide_local, local_counts), 'dp')  57.6 us
  transfers between devices with their start and end apart: 2, of which 2 were waited for; matrix products, arithmetic and copies ran while one was open for 2% of the time, Pallas kernels for 0%

profile of v1, /device:TPU:2, one launch (start us, length us, event | category | flops | bytes accessed | tf_op | source)
XLA Modules:
  0.0 642.6 jit_solution(6151923051783647887)
XLA Ops:
  7.2 0.0 all-reduce.2.cloned.1.call-start
  7.2 1.2 copy.7
  8.5 1.1 stack.2
  9.6 0.0 copy-start.2
  9.6 381.2 %all_to_all.5 = bf16[16,1024,256]{1,2,0:T(8,128)(2,1)S(1)} all-to-all(bf16[16,1024,256]{1,2,0:T(8,128)(2,1)S(1)} %stack.2), channel_id=1, replica_groups=mesh['dp'=32,'tensor'=16] {'tensor'}, dimensions={0} | all-to-all | bytes 16777216 | tf_op jit(solution)/shard_map/all_to_all | solution.py:19
  390.7 0.0 copy-start
  390.7 0.0 copy-start.1
  390.7 3.2 copy-done
  394.0 0.0 copy-done.2
  394.0 2.9 fusion
  396.9 0.0 all-reduce.2.cloned.1.call-update
  396.9 0.0 reduce-scatter.2.cloned.1.call-start
  397.0 0.0 copy-done.1
  397.0 7.7 %fusion.2 = f32[4096,256]{1,0:T(8,128)} fusion(bf16[1024,4096]{0,1:T(8,128)(2,1)} %bitcast.9, bf16[1024,256]{1,0:T(8,128)(2,1)S(1)} %copy-done.1), kind=kOutput, calls=%fused_computation.7 | convolution fusion | flops 2147483648 | bytes 13107200 | tf_op jit(solution)/shard_map/dot_general | solution.py:22
  404.7 0.0 reduce-scatter.2.cloned.1.call-update
  404.7 0.1 convert_reduce_fusion
  404.8 57.6 %psum.15 = f32[8]{0:T(128)S(1)} all-reduce(f32[8]{0:T(128)S(1)} %convert_reduce_fusion), channel_id=1, replica_groups=mesh['dp'=32,'tensor'=16] {'dp'}, use_global_device_ids=true, to_apply=%region_4.0 | all-reduce | flops 8 | bytes 64 | tf_op jit(solution)/shard_map/psum | solution.py:31
  462.5 61.7 %all-reduce.2.cloned.1.call-done = f32[8,4096]{1,0:T(8,128)} async-done(((f32[8,4096]{1,0:T(8,128)}), f32[8,4096]{1,0:T(8,128)}) %all-reduce.2.cloned.1.call-update) | async-done | bytes 131088 | tf_op jit(solution)/shard_map/psum | solution.py:31
  524.1 0.9 reduce_sum.18
  525.1 0.1 dynamic_slice.10
  525.2 0.1 dynamic_slice.9
  525.2 1.4 subtract_multiply_fusion
  526.6 107.4 %reduce-scatter.2.cloned.1.call-done = f32[128,256]{1,0:T(8,128)} async-done(((f32[4096,256]{1,0:T(8,128)}), f32[128,256]{1,0:T(8,128)}) %reduce-scatter.2.cloned.1.call-update) | async-done | bytes 131088 | tf_op jit(solution)/shard_map/reduce_scatter | solution.py:21
  634.0 1.0 bitcast_subtract_fusion
  635.0 0.8 copy.8
  (1 shorter events, 0.0 us)
Async XLA Ops:
  7.2 517.0 %all-reduce.2.cloned.1.call-start = ((), (), s32[]{:S(2)}) async-start(), calls=%async_computation.3 | async-start | bytes 262144 | tf_op jit(solution)/shard_map/psum | solution.py:31
  9.6 384.4 %copy-start.2 = (s32[1024]{0:T(1024)S(1)}, s32[1024]{0:T(1024)}, u32[]{:S(2)}) copy-start(s32[1024]{0:T(1024)} %param.3) | copy-start | bytes 12292
  390.7 3.2 copy-start
  390.7 6.2 copy-start.1
  396.9 237.1 %reduce-scatter.2.cloned.1.call-start = ((), (), s32[]{:S(2)}) async-start(), calls=%async_computation.2 | async-start | bytes 4325376 | tf_op jit(solution)/shard_map/reduce_scatter | solution.py:21
Sparse Core Ops, SparseCore 0:
  397.0 127.0 all-reduce.1
  528.6 105.3 reduce-scatter.1
